TPU v7x, 128 devices: a whole 4x4x4 slice. The times are simulated.
128 devices in a mesh: dp: 8 (over z, core), ctx: 16 (over x, y).
Axes of the slice: x: 4, y: 4, z: 4, core: 2. Of those that a mesh axis runs over, the one named last changes fastest.
Arguments:
- query_input: bfloat16 [8, 2048, 8192], P('dp', 'ctx'), may hold values from -12 to 12
- key_input: bfloat16 [8, 2048, 1024], P('dp', 'ctx'), may hold values from -12 to 12
- value_input: bfloat16 [8, 2048, 1024], P('dp', 'ctx'), may hold values from -6 to 6
- out_grad: bfloat16 [8, 2048, 8192], P('dp', 'ctx'), may hold values from -6 to 6
- query_bias: float32 [8192], replicated, may hold values from -1.75 to 1.75
- key_bias: float32 [1024], replicated, may hold values from -1.75 to 1.75
- value_bias: float32 [1024], replicated, may hold values from -1.75 to 1.75
- parents: int32 [8, 16], P('dp'), may hold values from 0 to 14, as said below
Outputs:
- attended: bfloat16 [8, 2048, 8192], P('dp', 'ctx')
- query_grad: float32 [8, 2048, 8192], P('dp', 'ctx')
- key_grad: float32 [8, 2048, 1024], P('dp', 'ctx')
- value_grad: float32 [8, 2048, 1024], P('dp', 'ctx')
- query_bias_grad: float32 [8192], replicated
- key_bias_grad: float32 [1024], replicated
- value_bias_grad: float32 [1024], replicated
Inputs may be any that keep to these rules, and one draw needn't show every extreme that they name: parents[t, 0] = 0 marks the root block; every other block's parent is an earlier block; the last block's parent is the block before it.
All inputs are finite; a program needn't handle non-finite values.
Results may differ from a plain program's by a relative error of at most 0.028.
Values may be sent and summed in bfloat16 or wider, within the bound.
No kernel may reach another device: no remote copies, remote signals or barrier semaphores. Data moves between devices by JAX's collectives and lax.ppermute only.
A program may use at most 128 MiB of HBM per device.

v0:
```python
import math

import jax
import jax.numpy as jnp
from jax import lax
from jax.sharding import PartitionSpec as P

Q_HEADS = 64
KV_HEADS = 8
HEAD = 128


LOG_BASE = math.log(1000000.0)
NEG_LARGE = -1e30


def ancestry(parent_list):
    block_count = parent_list.shape[0]
    block_ids = jnp.arange(block_count, dtype=jnp.int32)
    step_matrix = ((parent_list[:, None] == block_ids[None, :]) & (block_ids[:, None] > 0)).astype(
        jnp.float32
    )
    identity = jnp.eye(block_count, dtype=jnp.float32)

    def advance(iteration, current):
        return identity + jnp.dot(step_matrix, current, precision=lax.Precision.HIGHEST)

    return lax.fori_loop(0, block_count, advance, identity)


def rotate(values, places, direction):
    half_width = values.shape[-1] // 2
    frequency = jnp.exp(
        jnp.arange(half_width, dtype=jnp.float32) * (-2.0 * LOG_BASE / values.shape[-1])
    )
    angles = places[..., None] * frequency
    cosine = jnp.cos(angles)[..., None, :]
    sine_part = direction * jnp.sin(angles)[..., None, :]
    first_half = values[..., :half_width]
    second = values[..., half_width:]
    return jnp.concatenate(
        [first_half * cosine - second * sine_part, second * cosine + first_half * sine_part],
        axis=-1,
    )


def allowed_tiles(reach_values, same_block, row_count):
    row_ids = jnp.arange(row_count, dtype=jnp.int32)
    causal = row_ids[None, :] <= row_ids[:, None]
    return (reach_values[:, None, None] > 0.5) & (jnp.logical_not(same_block) | causal)[None]


def tile_forward(carried, query_tile, key_tile, value_tile, allowed, score_scale):
    running_max, running_sum, accumulated = carried
    tile_mask = allowed[:, :, None, None, :]
    scores = (
        jnp.einsum("tqghd,tkgd->tqghk", query_tile, key_tile, preferred_element_type=jnp.float32)
        * score_scale
    )
    scores = jnp.where(tile_mask, scores, NEG_LARGE)
    new_max = jnp.maximum(running_max, jnp.max(scores, axis=-1))
    weights = jnp.where(tile_mask, jnp.exp(scores - new_max[..., None]), 0.0)
    factor = jnp.exp(running_max - new_max)
    new_sum = running_sum * factor + jnp.sum(weights, axis=-1)
    mixed_sum = jnp.einsum(
        "tqghk,tkgd->tqghd",
        weights.astype(jnp.bfloat16),
        value_tile,
        preferred_element_type=jnp.float32,
    )
    return (new_max, new_sum, accumulated * factor[..., None] + mixed_sum)


def tile_backward(
    query_tile, key_tile, value_tile, grad_tile, log_total, row_delta, allowed, score_scale
):
    tile_mask = allowed[:, :, None, None, :]
    scores = (
        jnp.einsum("tqghd,tkgd->tqghk", query_tile, key_tile, preferred_element_type=jnp.float32)
        * score_scale
    )
    scores = jnp.where(tile_mask, scores, NEG_LARGE)
    probabilities = jnp.where(tile_mask, jnp.exp(scores - log_total[..., None]), 0.0)
    grad_probs = jnp.einsum(
        "tqghd,tkgd->tqghk", grad_tile, value_tile, preferred_element_type=jnp.float32
    )
    grad_scores = probabilities * (grad_probs - row_delta[..., None])
    grad_low = grad_scores.astype(jnp.bfloat16)
    query_part = (
        jnp.einsum("tqghk,tkgd->tqghd", grad_low, key_tile, preferred_element_type=jnp.float32)
        * score_scale
    )
    key_part = (
        jnp.einsum("tqghk,tqghd->tkgd", grad_low, query_tile, preferred_element_type=jnp.float32)
        * score_scale
    )
    value_part = jnp.einsum(
        "tqghk,tqghd->tkgd",
        probabilities.astype(jnp.bfloat16),
        grad_tile,
        preferred_element_type=jnp.float32,
    )
    return (query_part, key_part, value_part)


def body(query_input, key_input, value_input, out_grad, query_bias, key_bias, value_bias, parents):
    tree_count, row_count, query_width = query_input.shape
    key_width = key_input.shape[2]
    score_scale = HEAD ** (-0.5)
    group_size = Q_HEADS // KV_HEADS
    devices = lax.axis_size("ctx")
    device_index = lax.axis_index("ctx")
    ancestors = jax.vmap(ancestry)(parents)
    block_depth = jnp.sum(ancestors, axis=2) - 1.0
    offsets = jnp.arange(row_count, dtype=jnp.float32)
    own_depth = lax.dynamic_index_in_dim(block_depth, device_index, 1, keepdims=False)
    own_places = own_depth[:, None] * row_count + offsets[None, :]
    own_reach = lax.dynamic_index_in_dim(ancestors, device_index, 1, keepdims=False)
    queries = rotate(
        (query_input.astype(jnp.float32) + query_bias).reshape(
            tree_count, row_count, Q_HEADS, HEAD
        ),
        own_places,
        1.0,
    ).astype(jnp.bfloat16)
    key_rows = rotate(
        (key_input.astype(jnp.float32) + key_bias).reshape(tree_count, row_count, KV_HEADS, HEAD),
        own_places,
        1.0,
    ).astype(jnp.bfloat16)
    value_rows = (value_input.astype(jnp.float32) + value_bias).astype(jnp.bfloat16)
    tree_length = row_count * devices
    query_tiles = queries.reshape(tree_count, row_count, KV_HEADS, group_size, HEAD)
    grad_tiles = out_grad.reshape(tree_count, row_count, KV_HEADS, group_size, HEAD)
    flat_keys = key_rows.reshape(tree_count, row_count, key_width)
    start_state = (
        jnp.full((tree_count, row_count, KV_HEADS, group_size), NEG_LARGE, jnp.float32),
        jnp.zeros((tree_count, row_count, KV_HEADS, group_size), jnp.float32),
        jnp.zeros((tree_count, row_count, KV_HEADS, group_size, HEAD), jnp.float32),
    )
    key_piece = lax.all_gather(flat_keys, "ctx", axis=1, tiled=True)
    value_piece = lax.all_gather(value_rows, "ctx", axis=1, tiled=True)

    def one_block(block_step, current):
        key_tile = lax.dynamic_slice_in_dim(
            key_piece, block_step * row_count, row_count, 1
        ).reshape(tree_count, row_count, KV_HEADS, HEAD)
        value_tile = lax.dynamic_slice_in_dim(
            value_piece, block_step * row_count, row_count, 1
        ).reshape(tree_count, row_count, KV_HEADS, HEAD)
        reach_values = own_reach[:, block_step]
        allowed = allowed_tiles(reach_values, block_step == device_index, row_count)

        def compute():
            return tile_forward(current, query_tiles, key_tile, value_tile, allowed, score_scale)

        return lax.cond(jnp.any(reach_values > 0.5), compute, lambda: current)

    running_max, running_sum, accumulated = lax.fori_loop(
        0, key_piece.shape[1] // row_count, one_block, start_state
    )
    out_tiles = (accumulated / running_sum[..., None]).astype(jnp.bfloat16)
    log_total = running_max + jnp.log(running_sum)
    row_delta = jnp.sum(grad_tiles.astype(jnp.float32) * out_tiles.astype(jnp.float32), axis=-1)
    grad_state = (
        jnp.zeros((tree_count, row_count, KV_HEADS, group_size, HEAD), jnp.float32),
        jnp.zeros((tree_count, tree_length, 2, key_width), jnp.float32),
    )
    fold_key_piece = lax.all_gather(flat_keys, "ctx", axis=1, tiled=True)
    fold_value_piece = lax.all_gather(value_rows, "ctx", axis=1, tiled=True)

    def one_block(block_step, current):
        query_sum, key_grads = current
        key_block = block_step
        key_tile = lax.dynamic_slice_in_dim(
            fold_key_piece, block_step * row_count, row_count, 1
        ).reshape(tree_count, row_count, KV_HEADS, HEAD)
        value_tile = lax.dynamic_slice_in_dim(
            fold_value_piece, block_step * row_count, row_count, 1
        ).reshape(tree_count, row_count, KV_HEADS, HEAD)
        reach_values = own_reach[:, key_block]
        allowed = allowed_tiles(reach_values, key_block == device_index, row_count)

        def compute():
            query_part, key_part, value_part = tile_backward(
                query_tiles,
                key_tile,
                value_tile,
                grad_tiles,
                log_total,
                row_delta,
                allowed,
                score_scale,
            )
            stacked = jnp.stack(
                [
                    key_part.reshape(tree_count, row_count, key_width),
                    value_part.reshape(tree_count, row_count, key_width),
                ],
                axis=2,
            )
            return (
                query_sum + query_part,
                lax.dynamic_update_slice_in_dim(key_grads, stacked, key_block * row_count, 1),
            )

        return lax.cond(jnp.any(reach_values > 0.5), compute, lambda: current)

    query_sum, key_grads = lax.fori_loop(
        0, fold_key_piece.shape[1] // row_count, one_block, grad_state
    )
    own_grads = lax.psum_scatter(key_grads, "ctx", scatter_dimension=1, tiled=True)
    key_full = rotate(
        own_grads[:, :, 0].reshape(tree_count, row_count, KV_HEADS, HEAD), own_places, -1.0
    ).reshape(tree_count, row_count, key_width)
    value_full = own_grads[:, :, 1]
    query_full = rotate(
        query_sum.reshape(tree_count, row_count, Q_HEADS, HEAD), own_places, -1.0
    ).reshape(tree_count, row_count, query_width)
    attended = out_tiles.reshape(tree_count, row_count, query_width)
    query_total = jnp.sum(query_full, axis=(0, 1))
    key_total = jnp.sum(key_full, axis=(0, 1))
    value_total = jnp.sum(value_full, axis=(0, 1))
    query_total, key_total, value_total = lax.psum(
        (query_total, key_total, value_total), ("dp", "ctx")
    )
    return (attended, query_full, key_full, value_full, query_total, key_total, value_total)


def solution(mesh):
    placed = (
        P("dp", "ctx", None),
        P("dp", "ctx", None),
        P("dp", "ctx", None),
        P("dp", "ctx", None),
        P(),
        P(),
        P(),
        P("dp", None),
    )
    return jax.shard_map(
        body,
        mesh=mesh,
        in_specs=placed,
        out_specs=(
            P("dp", "ctx", None),
            P("dp", "ctx", None),
            P("dp", "ctx", None),
            P("dp", "ctx", None),
            P(),
            P(),
            P(),
        ),
        check_vma=False,
    )
```

profile of v0, /device:TPU:1, one launch (start us, length us, event | category | flops | bytes accessed | tf_op | source)
XLA Modules:
  0.0 708.9 jit_solution(4852979424388412003)
XLA Ops:
  7.3 14.0 %while.45 = (s32[]{:T(128)}, f32[1,16,16]{2,1,0:T(8,128)S(1)}, s32[16]{0:T(128)}, pred[16]{0:T(512)(128)(4,1)S(1)}, s32[]{:T(128)}) while((s32[]{:T(128)}, f32[1,16,16]{2,1,0:T(8,128)S(1)}, s32[16]{0:T(128)}, pred[16]{0:T(512)(128)(4,1)S(1)}, s32[]{:T(128)}) %tuple.173), condition=%wide.region_1.0_spmd.clone, body=%wide.region_0.0_spmd.clone.sunk | while | flops 50690 | bytes 4237 | solution.py:28
  27.9 2.9 subtract_convert_fusion
  30.8 3.3 copy.41
  34.1 2.9 copy.42
  38.5 2.7 copy.44
  41.2 4.1 copy.46
  45.2 38.9 %all-gather.3.cloned.1.call-done = bf16[1,2048,1024]{1,2,0:T(8,128)(2,1)} async-done(((bf16[1,128,1024]{1,2,0:T(8,128)(2,1)}), bf16[1,2048,1024]{1,2,0:T(8,128)(2,1)}) %all-gather.3.cloned.1.call-update) | async-done | bytes 4194320 | tf_op jit(solution)/shard_map/all_gather | solution.py:141
  84.2 58.8 %all-gather.5.cloned.1.call-done = bf16[1,2048,1024]{1,2,0:T(8,128)(2,1)} async-done(((bf16[1,128,1024]{1,2,0:T(8,128)(2,1)}), bf16[1,2048,1024]{1,2,0:T(8,128)(2,1)}) %all-gather.5.cloned.1.call-update) | async-done | bytes 4194320 | tf_op jit(solution)/shard_map/all_gather | solution.py:142
  143.0 2.5 broadcast.254.clone
  145.5 29.2 %while.43 = (s32[]{:T(128)}, f32[1,128,8,8]{1,3,2,0:T(8,128)S(1)}, f32[1,128,8,8]{1,3,2,0:T(8,128)S(1)}, f32[1,128,8,8,128]{1,4,3,2,0:T(8,128)}, f32[1,16]{1,0:T...) while((s32[]{:T(128)}, f32[1,128,8,8]{1,3,2,0:T(8,128)S(1)}, ...), condition=%wide.region_8.9_spmd, body=%wide.region_3.8_spmd.sunk | while | flops 552673280 | bytes 59048328 | solution.py:159
  146.8 8.4 %conditional.4 = ((f32[1,128,8,8]{1,3,2,0:T(8,128)S(1)}, f32[1,128,8,8]{1,3,2,0:T(8,128)S(1)}, f32[1,128,8,8,128]{1,4,3,2,0:T(8,128)})) conditional(s32[]{:T(128)} %bitcast.200, (f32[1,128,8,8]{1,3,2,0:T(8,128)S(1)}, f32[1,128,8,8]{1,3,2,0:T(8,128)S(1)}, f32[1,128,8,8,128]{1,4,3,2,0:T(8,128)}) %tuple.136, (f32[1,1]{1,0:T(1,128)}, s32[]{:T(128)}, ...), branch_computations={%region_4.4_spmd, %region_5.0_spmd} | conditional | flops 552673280 | bytes 58917024 | solution.py:157
  148.7 2.6 fusion.4
  151.4 1.8 bitcast_add_fusion
  174.7 5.3 multiply_reduce_fusion
  180.0 7.9 %broadcast_in_dim.123 = f32[1,2048,2,1024]{1,3,2,0:T(8,128)} broadcast(f32[]{:T(128)} %constant.227.clone.1), dimensions={} | broadcast | bytes 16777220 | tf_op jit(solution)/shard_map/broadcast_in_dim | solution.py:167
  187.9 2.5 broadcast.254
  190.4 37.6 %while.44 = (s32[]{:T(128)}, f32[1,128,8,8,128]{1,4,3,2,0:T(8,128)}, f32[1,2048,2,1024]{1,3,2,0:T(8,128)}, f32[1,16]{1,0:T(1,128)S(1)}, bf16[1,2048,1024]{1,2,0:...) while((s32[]{:T(128)}, ...), condition=%wide.region_13.14_spmd, body=%wide.region_10.13_spmd.sunk | while | flops 1357299712 | bytes 99762648 | solution.py:209
  191.7 16.9 %conditional.5 = ((f32[1,128,8,8,128]{1,4,3,2,0:T(8,128)}, f32[1,2048,2,1024]{1,3,2,0:T(8,128)})) conditional(s32[]{:T(128)} %bitcast.201, (f32[1,128,8,8,128]{1,4,3,2,0:T(8,128)}, f32[1,2048,2,1024]{1,3,2,0:T(8,128)}) %tuple.140, (s32[]{:T(128)}, bf16[1,2048,1024]{1,2,0:T(8,128)(2,1)}, f32[1,1]{1,0:T(1,128)}, s32[]{:T(128)}, ...), branch_computations={%region_11.11_spmd, %region_12.12_spmd} | conditional | flops 1357299712 | bytes 99631320 | solution.py:207
  192.8 2.7 fusion.35
  196.2 4.5 fusion.21
  206.6 2.0 copy-done.3
  228.0 18.0 %copy.49 = f32[1,2048,2,1024]{3,1,2,0:T(8,128)} copy(f32[1,2048,2,1024]{1,3,2,0:T(8,128)} %get-tuple-element.769) | data formatting | bytes 33554432 | tf_op jit(solution)/shard_map/while | solution.py:209
  246.0 4.0 fusion.68
  250.0 5.6 copy.70
  255.6 4.5 copy.71
  260.1 4.8 multiply_subtract_fusion
  264.9 3.1 fusion.65
  268.0 5.1 reshape.627
  273.1 2.9 copy.69
  275.9 357.7 %reduce-scatter.2.cloned.1.call-done = f32[1,128,2,1024]{3,1,2,0:T(8,128)} async-done(((f32[1,2048,2,1024]{3,1,2,0:T(8,128)}), f32[1,128,2,1024]{3,1,2,0:T(8,128)}) %reduce-scatter.2.cloned.1.call-update) | async-done | bytes 1048592 | tf_op jit(solution)/shard_map/reduce_scatter | solution.py:212
  633.7 2.1 slice_reduce_fusion
  637.2 65.2 %all-reduce = (f32[8192]{0:T(1024)}, f32[1024]{0:T(1024)}, f32[1024]{0:T(1024)}) all-reduce(f32[8192]{0:T(1024)S(1)} %bitcast.225, f32[1024]{0:T(1024)S(1)} %bitcast.230, f32[1024]{0:T(1024)S(1)} %get-tuple-element.876), channel_id=1, replica_groups=mesh['dp'=8,'ctx'=16] {'dp','ctx'}, use_global_device_ids=true, to_apply=%region_16.17 | all-reduce | flops 10240 | bytes 81920 | tf_op jit(solution)/shard_map/psum | solution.py:224
  (223 shorter events, 52.6 us)
Async XLA Ops:
  7.2 18.4 %copy-start.8 = (bf16[1,128,1024]{2,1,0:T(8,128)(2,1)S(1)}, bf16[1,128,1024]{2,1,0:T(8,128)(2,1)}, u32[]{:S(2)}) copy-start(bf16[1,128,1024]{2,1,0:T(8,128)(2,1)} %param.20) | copy-start | bytes 786436
  7.2 18.6 %copy-start.10 = (f32[1024]{0:T(1024)S(1)}, f32[1024]{0:T(1024)}, u32[]{:S(2)}) copy-start(f32[1024]{0:T(1024)} %param.24) | copy-start | bytes 12292
  7.2 19.5 %copy-start.7 = (bf16[1,128,8192]{2,1,0:T(8,128)(2,1)S(1)}, bf16[1,128,8192]{2,1,0:T(8,128)(2,1)}, u32[]{:S(2)}) copy-start(bf16[1,128,8192]{2,1,0:T(8,128)(2,1)} %param.18) | copy-start | bytes 6291460
  7.2 19.5 %copy-start.9 = (f32[8192]{0:T(1024)S(1)}, f32[8192]{0:T(1024)}, u32[]{:S(2)}) copy-start(f32[8192]{0:T(1024)} %param.22) | copy-start | bytes 98308
  7.2 77.0 %all-gather.3.cloned.1.call-start = ((), (), s32[]{:S(2)}) async-start(), calls=%async_computation.1 | async-start | bytes 4456448 | tf_op jit(solution)/shard_map/all_gather | solution.py:141
  25.5 117.5 %all-gather.5.cloned.1.call-start = ((), (), s32[]{:S(2)}) async-start(), calls=%async_computation.2 | async-start | bytes 4456448 | tf_op jit(solution)/shard_map/all_gather | solution.py:142
  26.7 607.0 %reduce-scatter.2.cloned.1.call-start = ((), (), s32[]{:S(2)}) async-start(), calls=%async_computation.3 | async-start | bytes 17825792 | tf_op jit(solution)/shard_map/reduce_scatter | solution.py:212
  147.9 3.5 copy-start
  153.1 2.0 copy-start.1
  196.2 5.3 copy-start.5
  200.7 2.2 copy-start.4
  202.9 2.3 copy-start.2
  206.5 2.0 copy-start.3
  268.0 5.1 copy-start.6
Sparse Core Ops, SparseCore 0:
  25.6 58.4 all-gather.2
  86.9 56.0 all-gather.4
  246.1 387.4 reduce-scatter.1
where the time goes:
time: 711 us; the launch traced here: 709 us
  waiting for transfers between devices  455 us (64%)
  local copies, waits for them, and re-layouts  76.4 us (11%)
  blocking collectives  65.2 us (9%)
  other arithmetic  44.5 us (6%)
  matrix products  28.8 us (4%)
  loops' own time  23.8 us (3%)
  between operations  14.6 us (2%)
    reduce_scatter x1, waiting for transfers between devices, body(): lax.psum_scatter(key_grads, 'ctx', scatter_dimension=1, tiled=True)  358 us
    psum x1, blocking collectives, body(): lax.psum((query_total, key_total, value_total), ('dp', 'ctx'))  65.2 us
    all_gather x1, waiting for transfers between devices, body(): value_piece = lax.all_gather(value_rows, 'ctx', axis=1, tiled=True)  58.8 us
    all_gather x1, waiting for transfers between devices, body(): key_piece = lax.all_gather(flat_keys, 'ctx', axis=1, tiled=True)  38.9 us
    gt x32, other arithmetic, one_block(): return lax.cond(jnp.any(reach_values > 0.5), compute, lambda: current)  18.8 us
    while x1, local copies, waits for them, and re-layouts, body(): lax.fori_loop(0, fold_key_piece.shape[1] // row_count, one_block, grad_st...  18 us
    unnamed x17, local copies, waits for them, and re-layouts  15.2 us
  transfers between devices with their start and end apart: 3, of which 3 were waited for; matrix products, arithmetic and copies ran while one was open for 7% of the time, Pallas kernels for 0%

commit v1 on v0

--- a/solution.py
+++ b/solution.py
@@ -20,12 +20,12 @@
     step_matrix = ((parent_list[:, None] == block_ids[None, :]) & (block_ids[:, None] > 0)).astype(
         jnp.float32
     )
-    identity = jnp.eye(block_count, dtype=jnp.float32)
-
-    def advance(iteration, current):
-        return identity + jnp.dot(step_matrix, current, precision=lax.Precision.HIGHEST)
-
-    return lax.fori_loop(0, block_count, advance, identity)
+    reach = jnp.eye(block_count, dtype=jnp.float32) + step_matrix
+    steps = 1
+    while steps < block_count:
+        reach = jnp.minimum(jnp.dot(reach, reach, precision=lax.Precision.HIGHEST), 1.0)
+        steps *= 2
+    return reach
 
 
 def rotate(values, places, direction):
@@ -110,11 +110,13 @@
     group_size = Q_HEADS // KV_HEADS
     devices = lax.axis_size("ctx")
     device_index = lax.axis_index("ctx")
+    raw_pair = jnp.stack([key_input, value_input], axis=2)
+    gathered = lax.all_gather(raw_pair, "ctx", axis=1, tiled=True)
     ancestors = jax.vmap(ancestry)(parents)
     block_depth = jnp.sum(ancestors, axis=2) - 1.0
     offsets = jnp.arange(row_count, dtype=jnp.float32)
-    own_depth = lax.dynamic_index_in_dim(block_depth, device_index, 1, keepdims=False)
-    own_places = own_depth[:, None] * row_count + offsets[None, :]
+    all_places = block_depth[:, :, None] * row_count + offsets[None, None, :]
+    own_places = lax.dynamic_index_in_dim(all_places, device_index, 1, keepdims=False)
     own_reach = lax.dynamic_index_in_dim(ancestors, device_index, 1, keepdims=False)
     queries = rotate(
         (query_input.astype(jnp.float32) + query_bias).reshape(
@@ -123,31 +125,31 @@
         own_places,
         1.0,
     ).astype(jnp.bfloat16)
-    key_rows = rotate(
-        (key_input.astype(jnp.float32) + key_bias).reshape(tree_count, row_count, KV_HEADS, HEAD),
-        own_places,
+    tree_length = row_count * devices
+    flat_places = all_places.reshape(tree_count, tree_length)
+    key_piece = rotate(
+        (gathered[:, :, 0].astype(jnp.float32) + key_bias).reshape(
+            tree_count, tree_length, KV_HEADS, HEAD
+        ),
+        flat_places,
         1.0,
     ).astype(jnp.bfloat16)
-    value_rows = (value_input.astype(jnp.float32) + value_bias).astype(jnp.bfloat16)
-    tree_length = row_count * devices
+    value_piece = (
+        (gathered[:, :, 1].astype(jnp.float32) + value_bias)
+        .astype(jnp.bfloat16)
+        .reshape(tree_count, tree_length, KV_HEADS, HEAD)
+    )
     query_tiles = queries.reshape(tree_count, row_count, KV_HEADS, group_size, HEAD)
     grad_tiles = out_grad.reshape(tree_count, row_count, KV_HEADS, group_size, HEAD)
-    flat_keys = key_rows.reshape(tree_count, row_count, key_width)
     start_state = (
         jnp.full((tree_count, row_count, KV_HEADS, group_size), NEG_LARGE, jnp.float32),
         jnp.zeros((tree_count, row_count, KV_HEADS, group_size), jnp.float32),
         jnp.zeros((tree_count, row_count, KV_HEADS, group_size, HEAD), jnp.float32),
     )
-    key_piece = lax.all_gather(flat_keys, "ctx", axis=1, tiled=True)
-    value_piece = lax.all_gather(value_rows, "ctx", axis=1, tiled=True)
 
     def one_block(block_step, current):
-        key_tile = lax.dynamic_slice_in_dim(
-            key_piece, block_step * row_count, row_count, 1
-        ).reshape(tree_count, row_count, KV_HEADS, HEAD)
-        value_tile = lax.dynamic_slice_in_dim(
-            value_piece, block_step * row_count, row_count, 1
-        ).reshape(tree_count, row_count, KV_HEADS, HEAD)
+        key_tile = lax.dynamic_slice_in_dim(key_piece, block_step * row_count, row_count, 1)
+        value_tile = lax.dynamic_slice_in_dim(value_piece, block_step * row_count, row_count, 1)
         reach_values = own_reach[:, block_step]
         allowed = allowed_tiles(reach_values, block_step == device_index, row_count)
 
@@ -156,30 +158,17 @@
 
         return lax.cond(jnp.any(reach_values > 0.5), compute, lambda: current)
 
-    running_max, running_sum, accumulated = lax.fori_loop(
-        0, key_piece.shape[1] // row_count, one_block, start_state
-    )
+    running_max, running_sum, accumulated = lax.fori_loop(0, devices, one_block, start_state)
     out_tiles = (accumulated / running_sum[..., None]).astype(jnp.bfloat16)
     log_total = running_max + jnp.log(running_sum)
     row_delta = jnp.sum(grad_tiles.astype(jnp.float32) * out_tiles.astype(jnp.float32), axis=-1)
-    grad_state = (
-        jnp.zeros((tree_count, row_count, KV_HEADS, group_size, HEAD), jnp.float32),
-        jnp.zeros((tree_count, tree_length, 2, key_width), jnp.float32),
-    )
-    fold_key_piece = lax.all_gather(flat_keys, "ctx", axis=1, tiled=True)
-    fold_value_piece = lax.all_gather(value_rows, "ctx", axis=1, tiled=True)
-
-    def one_block(block_step, current):
-        query_sum, key_grads = current
-        key_block = block_step
-        key_tile = lax.dynamic_slice_in_dim(
-            fold_key_piece, block_step * row_count, row_count, 1
-        ).reshape(tree_count, row_count, KV_HEADS, HEAD)
-        value_tile = lax.dynamic_slice_in_dim(
-            fold_value_piece, block_step * row_count, row_count, 1
-        ).reshape(tree_count, row_count, KV_HEADS, HEAD)
-        reach_values = own_reach[:, key_block]
-        allowed = allowed_tiles(reach_values, key_block == device_index, row_count)
+
+    def one_grad_block(query_sum, block_step):
+        key_tile = lax.dynamic_slice_in_dim(key_piece, block_step * row_count, row_count, 1)
+        value_tile = lax.dynamic_slice_in_dim(value_piece, block_step * row_count, row_count, 1)
+        block_places = lax.dynamic_index_in_dim(all_places, block_step, 1, keepdims=False)
+        reach_values = own_reach[:, block_step]
+        allowed = allowed_tiles(reach_values, block_step == device_index, row_count)
 
         def compute():
             query_part, key_part, value_part = tile_backward(
@@ -192,35 +181,40 @@
                 allowed,
                 score_scale,
             )
-            stacked = jnp.stack(
-                [
-                    key_part.reshape(tree_count, row_count, key_width),
-                    value_part.reshape(tree_count, row_count, key_width),
-                ],
-                axis=2,
-            )
-            return (
-                query_sum + query_part,
-                lax.dynamic_update_slice_in_dim(key_grads, stacked, key_block * row_count, 1),
-            )
-
-        return lax.cond(jnp.any(reach_values > 0.5), compute, lambda: current)
-
-    query_sum, key_grads = lax.fori_loop(
-        0, fold_key_piece.shape[1] // row_count, one_block, grad_state
-    )
-    own_grads = lax.psum_scatter(key_grads, "ctx", scatter_dimension=1, tiled=True)
-    key_full = rotate(
-        own_grads[:, :, 0].reshape(tree_count, row_count, KV_HEADS, HEAD), own_places, -1.0
-    ).reshape(tree_count, row_count, key_width)
+            key_back = rotate(key_part, block_places, -1.0)
+            return (query_sum + query_part, key_back, value_part)
+
+        def skip():
+            zeros = jnp.zeros((tree_count, row_count, KV_HEADS, HEAD), jnp.float32)
+            return (query_sum, zeros, zeros)
+
+        new_sum, key_back, value_part = lax.cond(jnp.any(reach_values > 0.5), compute, skip)
+        return new_sum, (key_back, value_part)
+
+    query_sum, (key_parts, value_parts) = lax.scan(
+        one_grad_block,
+        jnp.zeros((tree_count, row_count, KV_HEADS, group_size, HEAD), jnp.float32),
+        jnp.arange(devices, dtype=jnp.int32),
+    )
+    key_total = jnp.sum(key_parts, axis=(0, 1, 2)).reshape(key_width)
+    value_total = jnp.sum(value_parts, axis=(0, 1, 2)).reshape(key_width)
+    stacked = jnp.stack(
+        [
+            key_parts.reshape(devices, tree_count, row_count, key_width),
+            value_parts.reshape(devices, tree_count, row_count, key_width),
+        ],
+        axis=3,
+    ).astype(jnp.bfloat16)
+    own_grads = lax.psum_scatter(stacked, "ctx", scatter_dimension=0, tiled=True)[0].astype(
+        jnp.float32
+    )
+    key_full = own_grads[:, :, 0]
     value_full = own_grads[:, :, 1]
     query_full = rotate(
         query_sum.reshape(tree_count, row_count, Q_HEADS, HEAD), own_places, -1.0
     ).reshape(tree_count, row_count, query_width)
     attended = out_tiles.reshape(tree_count, row_count, query_width)
     query_total = jnp.sum(query_full, axis=(0, 1))
-    key_total = jnp.sum(key_full, axis=(0, 1))
-    value_total = jnp.sum(value_full, axis=(0, 1))
     query_total, key_total, value_total = lax.psum(
         (query_total, key_total, value_total), ("dp", "ctx")
     )

time: 711 us -> 674 us (0.948)
  waiting for transfers between devices: 455 us -> 46.6 us
  blocking collectives: 65.2 us -> 325 us
  local copies, waits for them, and re-layouts: 76.4 us -> 131 us
  other arithmetic: 44.5 us -> 84.4 us
  loops' own time: 23.8 us -> 57 us
  matrix products: 28.8 us -> 14.5 us
    reduce_scatter x1 -> x0, waiting for transfers between devices: 358 us -> none  [body(): lax.psum_scatter(key_grads, 'ctx', scatter_dimension=1, tiled=True)]
    psum x1, blocking collectives: 65.2 us -> 325 us  [body(): lax.psum((query_total, key_total, value_total), ('dp', 'ctx'))]
    all_gather x2 -> x1, waiting for transfers between devices: 97.7 us -> 46.5 us  [body(): gathered = lax.all_gather(raw_pair, 'ctx', axis=1, tiled=True)]
    another operation x3 -> x18, loops' own time: 21.7 us -> 55.9 us  [the longest x1 42.2 us: body(): lax.scan(one_grad_block, jnp.zeros((tree_count, row_count, KV_HEADS, grou...]
    dynamic_update_slice x0 -> x32, local copies, waits for them, and re-layouts: none -> 27.1 us  [body(): lax.scan(one_grad_block, jnp.zeros((tree_count, row_count, KV_HEADS, grou...]
    another operation x5 -> x7, local copies, waits for them, and re-layouts: 11.9 us -> 30.5 us
    unnamed x17 -> x27, local copies, waits for them, and re-layouts: 15.2 us -> 32.4 us
    reduce_sum x3 -> x2, other arithmetic: 2.43 us -> 16.2 us  [the longest x1 9.07 us: body(): key_total = jnp.sum(key_parts, axis=(0, 1, 2)).reshape(key_width)]
  transfers between devices with their start and end apart: 3 -> 2, of which waited for: 3 -> 1; matrix products, arithmetic and copies ran while one was open for 7% -> 9% of each run, Pallas kernels for 0% -> 0%
where the time goes in v1:
time: 674 us; the launch traced here: 673 us
  blocking collectives  325 us (48%)
  local copies, waits for them, and re-layouts  131 us (19%)
  other arithmetic  84.4 us (13%)
  loops' own time  57 us (8%)
  waiting for transfers between devices  46.6 us (7%)
  between operations  14.7 us (2%)
  matrix products  14.5 us (2%)
    psum x1, blocking collectives, body(): lax.psum((query_total, key_total, value_total), ('dp', 'ctx'))  325 us
    all_gather x1, waiting for transfers between devices, body(): gathered = lax.all_gather(raw_pair, 'ctx', axis=1, tiled=True)  46.5 us
    another operation x1, loops' own time, body(): lax.scan(one_grad_block, jnp.zeros((tree_count, row_count, KV_HEADS, grou...  42.2 us
    unnamed x27, local copies, waits for them, and re-layouts  32.4 us
    dynamic_update_slice x32, local copies, waits for them, and re-layouts, body(): lax.scan(one_grad_block, jnp.zeros((tree_count, row_count, KV_HEADS, grou...  27.1 us
    another operation x5, local copies, waits for them, and re-layouts  16.9 us
    another operation x2, local copies, waits for them, and re-layouts, body(): jnp.stack([key_parts.reshape(devices, tree_count, row_count, key_width),...  13.6 us
  transfers between devices with their start and end apart: 2, of which 1 were waited for; matrix products, arithmetic and copies ran while one was open for 9% of the time, Pallas kernels for 0%

profile of v1, /device:TPU:1, one launch (start us, length us, event | category | flops | bytes accessed | tf_op | source)
XLA Modules:
  0.0 673.3 jit_solution(2253495514434636695)
XLA Ops:
  10.4 3.2 copy.66
  13.7 2.7 copy.70
  18.4 2.8 copy.97
  24.2 6.6 subtract_convert_fusion
  30.8 3.3 copy.62
  34.1 2.9 copy.63
  43.1 46.5 %all-gather.2.cloned.1.call-done = bf16[1,2048,2,1024]{1,3,2,0:T(8,128)(2,1)} async-done(((bf16[1,128,2,1024]{1,3,2,0:T(8,128)(2,1)}), bf16[1,2048,2,1024]{1,3,2,0:T(8,128)(2,1)}) %all-gather.2.cloned.1.call-update) | async-done | bytes 8388624 | tf_op jit(solution)/shard_map/all_gather | solution.py:114
  89.7 5.3 fusion.89
  99.6 6.5 copy.64
  106.1 4.9 fusion.81
  111.0 6.7 copy.69
  120.3 29.7 %while.35 = (s32[]{:T(128)}, f32[1,128,8,8]{1,3,2,0:T(8,128)S(1)}, f32[1,128,8,8]{1,3,2,0:T(8,128)S(1)}, f32[1,128,8,8,128]{1,4,3,2,0:T(8,128)}, f32[1,16]{1,0:T...) while((s32[]{:T(128)}, f32[1,128,8,8]{1,3,2,0:T(8,128)S(1)}, ...), condition=%wide.region_6.7_spmd, body=%wide.region_1.6_spmd.sunk | while | flops 552673280 | bytes 57999760 | solution.py:161
  121.6 8.3 %conditional.5 = ((f32[1,128,8,8]{1,3,2,0:T(8,128)S(1)}, f32[1,128,8,8]{1,3,2,0:T(8,128)S(1)}, f32[1,128,8,8,128]{1,4,3,2,0:T(8,128)})) conditional(s32[]{:T(128)} %bitcast.227, (f32[1,128,8,8]{1,3,2,0:T(8,128)S(1)}, f32[1,128,8,8]{1,3,2,0:T(8,128)S(1)}, f32[1,128,8,8,128]{1,4,3,2,0:T(8,128)}) %tuple.130, (f32[1,1]{1,0:T(1,128)}, s32[]{:T(128)}, ...), branch_computations={%region_2.2_spmd, %region_3.0_spmd} | conditional | flops 552673280 | bytes 57868452 | solution.py:159
  122.4 2.7 fusion.2
  125.1 2.7 bitcast_add_fusion
  150.0 5.3 multiply_reduce_fusion
  157.8 106.4 %while.36 = (s32[]{:T(128)}, f32[1,128,8,8,128]{1,4,3,2,0:T(8,128)}, f32[16,1,128,8,128]{2,4,3,1,0:T(8,128)}, f32[16,1,128,8,128]{4,2,3,1,0:T(8,128)}, s32[16]{0...) while((s32[]{:T(128)}, ...), condition=%wide.region_11.12_spmd.clone, body=%wide.region_8.11_spmd.clone.sunk | while | flops 1357578368 | bytes 84175408 | solution.py:194
  161.7 15.5 %conditional.6 = (f32[1,128,8,8,128]{1,4,3,2,0:T(8,128)}, f32[1,1,128,8,128]{2,4,3,1,0:T(8,128)S(1)}, f32[1,1,128,8,128]{4,2,3,1,0:T(8,128)S(1)}) conditional(s32[]{:T(128)} %bitcast.229, f32[1,128,8,8,128]{1,4,3,2,0:T(8,128)} %get-tuple-element.1072, (s32[]{:T(128)}, bf16[1,2048,8,128]{3,1,2,0:T(8,128)(2,1)}, f32[1,1]{1,0:T(1,128)}, s32[]{:T(128)}, ...), branch_computations={%region_9.9_spmd, %region_10.10_spmd} | conditional | flops 1357578368 | bytes 81938640 | solution.py:191
  264.2 7.2 %fusion.87 = (f32[8,128]{1,0:T(8,128)S(1)}, bf16[16,1,128,8,128]{4,2,3,1,0:T(8,128)(2,1)S(1)}) fusion(f32[16,1,128,8,128]{4,2,3,1,0:T(8,128)} %get-tuple-element.634), kind=kLoop, calls=%fused_computation.127 | loop fusion | flops 4193280 | bytes 12587008 | tf_op jit(solution)/shard_map/reduce_sum | solution.py:200
  271.4 5.5 copy.74
  276.9 7.3 %stack.20 = bf16[16,1,128,1,1024]{4,2,3,1,0:T(8,128)(2,1)} reshape(bf16[16,1,128,8,128]{4,3,2,0,1:T(8,128)(2,1)} %copy.74) | data formatting | bytes 8388608 | tf_op jit(solution)/shard_map/stack | solution.py:201
  284.2 9.1 %fusion.88 = (f32[8,128]{1,0:T(8,128)S(1)}, bf16[16,1,128,8,128]{2,4,3,1,0:T(8,128)(2,1)}) fusion(f32[16,1,128,8,128]{2,4,3,1,0:T(8,128)} %get-tuple-element.633), kind=kLoop, calls=%fused_computation.128 | loop fusion | flops 4193280 | bytes 12587008 | tf_op jit(solution)/shard_map/reduce_sum | solution.py:199
  293.3 6.3 copy.89
  299.6 7.5 %pad_maximum_fusion = bf16[16,1,128,2,1024]{4,2,3,1,0:T(8,128)(2,1)} fusion(bf16[16,1,128,1,1024]{4,2,3,1,0:T(8,128)(2,1)} %stack.20, bf16[16,1,128,1,1024]{4,2,3,1,0:T(8,128)(2,1)} %copy.89), kind=kLoop, calls=%fused_computation.84 | loop fusion | flops 4194304 | bytes 16777216 | tf_op jit(solution)/shard_map/stack | solution.py:201
  308.7 2.9 copy.75
  311.6 4.1 fusion.90
  315.6 5.5 copy.91
  321.2 4.8 copy.90
  326.0 4.8 multiply_subtract_fusion.1
  330.7 3.1 fusion.84
  333.9 4.9 reshape.987
  338.8 325.0 %all-reduce.1 = (f32[8192]{0:T(1024)}, f32[1024]{0:T(1024)}, f32[1024]{0:T(1024)}) all-reduce(f32[8192]{0:T(1024)S(1)} %bitcast.245, f32[1024]{0:T(1024)S(1)} %bitcast.253, f32[1024]{0:T(1024)S(1)} %bitcast.252), channel_id=1, replica_groups=mesh['dp'=8,'ctx'=16] {'dp','ctx'}, use_global_device_ids=true, to_apply=%region_14.15 | all-reduce | flops 10240 | bytes 81920 | tf_op jit(solution)/shard_map/psum | solution.py:218
  (304 shorter events, 103.4 us)
Async XLA Ops:
  7.2 82.5 %all-gather.2.cloned.1.call-start = ((), (), s32[]{:S(2)}) async-start(), calls=%async_computation.1 | async-start | bytes 8912896 | tf_op jit(solution)/shard_map/all_gather | solution.py:114
  10.3 653.5 %reduce-scatter.4.cloned.1.call-start = ((), (), s32[]{:S(2)}) async-start(), calls=%async_computation.2 | async-start | bytes 8912896
  10.4 6.0 copy-start.10
  13.7 4.8 copy-start.4
  18.4 2.8 copy-start.13
  24.2 6.6 copy-start.7
  43.1 51.9 %copy-start.11 = (f32[1024]{0:T(1024)S(1)}, f32[1024]{0:T(1024)}, u32[]{:S(2)}) copy-start(f32[1024]{0:T(1024)} %param.21) | copy-start | bytes 12292
  99.6 6.5 copy-start.12
  121.6 3.5 copy-start
  127.8 2.0 copy-start.1
  163.6 3.2 copy-start.6
  170.3 2.2 copy-start.2
  175.1 2.0 copy-start.3
  307.1 1.6 copy-start.5
  321.2 4.8 copy-start.8
  321.2 4.8 copy-start.9
Sparse Core Ops, SparseCore 0:
  10.7 78.9 all-gather.1
  307.2 341.3 reduce-scatter.3

commit v2 on v1

v2 whole, which is shorter than its diff:
```python
import functools
import math

import jax
import jax.numpy as jnp
from jax import lax
from jax.experimental import pallas as pl
from jax.experimental.pallas import tpu as pltpu
from jax.sharding import PartitionSpec as P

Q_HEADS = 64
KV_HEADS = 8
HEAD = 128


LOG_BASE = math.log(1000000.0)
NEG_LARGE = -1e30


def ancestry(parent_list):
    block_count = parent_list.shape[0]
    block_ids = jnp.arange(block_count, dtype=jnp.int32)
    step_matrix = ((parent_list[:, None] == block_ids[None, :]) & (block_ids[:, None] > 0)).astype(
        jnp.float32
    )
    reach = jnp.eye(block_count, dtype=jnp.float32) + step_matrix
    steps = 1
    while steps < block_count:
        reach = jnp.minimum(jnp.dot(reach, reach, precision=lax.Precision.HIGHEST), 1.0)
        steps *= 2
    return reach


def rotate(values, places, direction):
    half_width = values.shape[-1] // 2
    frequency = jnp.exp(
        jnp.arange(half_width, dtype=jnp.float32) * (-2.0 * LOG_BASE / values.shape[-1])
    )
    angles = places[..., None] * frequency
    cosine = jnp.cos(angles)[..., None, :]
    sine_part = direction * jnp.sin(angles)[..., None, :]
    first_half = values[..., :half_width]
    second = values[..., half_width:]
    return jnp.concatenate(
        [first_half * cosine - second * sine_part, second * cosine + first_half * sine_part],
        axis=-1,
    )


def allowed_tiles(reach_values, same_block, row_count):
    row_ids = jnp.arange(row_count, dtype=jnp.int32)
    causal = row_ids[None, :] <= row_ids[:, None]
    return (reach_values[:, None, None] > 0.5) & (jnp.logical_not(same_block) | causal)[None]


def _visible(block, own, rows):
    row_ids = lax.broadcasted_iota(jnp.int32, (rows, rows), 0)
    col_ids = lax.broadcasted_iota(jnp.int32, (rows, rows), 1)
    return jnp.logical_or(block != own, col_ids <= row_ids)


def _fwd_kernel(reach_ref, own_ref, q_ref, k_ref, v_ref, o_ref, lse_ref, m_scr, l_scr, acc_scr,
                *, heads, head, scale):
    block = pl.program_id(1)
    last = pl.num_programs(1) - 1
    rows = q_ref.shape[0]

    @pl.when(block == 0)
    def _():
        m_scr[...] = jnp.full(m_scr.shape, NEG_LARGE, jnp.float32)
        l_scr[...] = jnp.zeros(l_scr.shape, jnp.float32)
        acc_scr[...] = jnp.zeros(acc_scr.shape, jnp.float32)

    @pl.when(reach_ref[block] > 0)
    def _():
        mask = _visible(block, own_ref[0], rows)
        key = k_ref[0]
        value = v_ref[0]
        for h in range(heads):
            query = q_ref[:, h * head:(h + 1) * head]
            scores = lax.dot_general(query, key, (((1,), (1,)), ((), ())),
                                     preferred_element_type=jnp.float32) * scale
            scores = jnp.where(mask, scores, NEG_LARGE)
            m_prev = m_scr[h]
            m_new = jnp.maximum(m_prev, jnp.max(scores, axis=-1, keepdims=True))
            weights = jnp.where(mask, jnp.exp(scores - m_new), 0.0)
            factor = jnp.exp(m_prev - m_new)
            l_scr[h] = l_scr[h] * factor + jnp.sum(weights, axis=-1, keepdims=True)
            mixed = jnp.dot(weights.astype(jnp.bfloat16), value, preferred_element_type=jnp.float32)
            acc_scr[h] = acc_scr[h] * factor + mixed
            m_scr[h] = m_new

    @pl.when(block == last)
    def _():
        for h in range(heads):
            total = l_scr[h]
            o_ref[:, h * head:(h + 1) * head] = (acc_scr[h] / total).astype(o_ref.dtype)
            lse_ref[h] = m_scr[h] + jnp.log(total)


def flash_forward(reach, own, queries, key_stack, value_stack, *, heads, head, scale, interpret=False):
    rows, width = queries.shape
    blocks = key_stack.shape[0]
    groups = width // (heads * head)
    kernel = functools.partial(_fwd_kernel, heads=heads, head=head, scale=scale)
    grid_spec = pltpu.PrefetchScalarGridSpec(
        num_scalar_prefetch=2,
        grid=(groups, blocks),
        in_specs=[
            pl.BlockSpec((rows, heads * head), lambda g, b, r, o: (0, g)),
            pl.BlockSpec((1, rows, head), lambda g, b, r, o: (b, 0, g)),
            pl.BlockSpec((1, rows, head), lambda g, b, r, o: (b, 0, g)),
        ],
        out_specs=[
            pl.BlockSpec((rows, heads * head), lambda g, b, r, o: (0, g)),
            pl.BlockSpec((heads, rows, 1), lambda g, b, r, o: (g, 0, 0)),
        ],
        scratch_shapes=[
            pltpu.VMEM((heads, rows, 1), jnp.float32),
            pltpu.VMEM((heads, rows, 1), jnp.float32),
            pltpu.VMEM((heads, rows, head), jnp.float32),
        ],
    )
    return pl.pallas_call(
        kernel,
        grid_spec=grid_spec,
        out_shape=[
            jax.ShapeDtypeStruct((rows, width), jnp.bfloat16),
            jax.ShapeDtypeStruct((groups * heads, rows, 1), jnp.float32),
        ],
        compiler_params=pltpu.CompilerParams(dimension_semantics=("arbitrary", "arbitrary")),
        interpret=interpret,
    )(reach, own, queries, key_stack, value_stack)


def _bwd_kernel(reach_ref, own_ref, q_ref, do_ref, k_ref, v_ref, lse_ref, delta_ref,
                dq_ref, dk_ref, dv_ref, dq_scr, *, heads, head, scale):
    block = pl.program_id(1)
    last = pl.num_programs(1) - 1
    rows = q_ref.shape[0]

    @pl.when(block == 0)
    def _():
        dq_scr[...] = jnp.zeros(dq_scr.shape, jnp.float32)

    @pl.when(reach_ref[block] > 0)
    def _():
        mask = _visible(block, own_ref[0], rows)
        key = k_ref[0]
        value = v_ref[0]
        key_acc = jnp.zeros((rows, head), jnp.float32)
        value_acc = jnp.zeros((rows, head), jnp.float32)
        for h in range(heads):
            query = q_ref[:, h * head:(h + 1) * head]
            grad = do_ref[:, h * head:(h + 1) * head]
            scores = lax.dot_general(query, key, (((1,), (1,)), ((), ())),
                                     preferred_element_type=jnp.float32) * scale
            scores = jnp.where(mask, scores, NEG_LARGE)
            probs = jnp.where(mask, jnp.exp(scores - lse_ref[h]), 0.0)
            grad_probs = lax.dot_general(grad, value, (((1,), (1,)), ((), ())),
                                         preferred_element_type=jnp.float32)
            grad_low = (probs * (grad_probs - delta_ref[h])).astype(jnp.bfloat16)
            dq_scr[h] = dq_scr[h] + jnp.dot(grad_low, key, preferred_element_type=jnp.float32) * scale
            key_acc = key_acc + lax.dot_general(grad_low, query, (((0,), (0,)), ((), ())),
                                                preferred_element_type=jnp.float32)
            value_acc = value_acc + lax.dot_general(probs.astype(jnp.bfloat16), grad,
                                                    (((0,), (0,)), ((), ())),
                                                    preferred_element_type=jnp.float32)
        dk_ref[0] = key_acc * scale
        dv_ref[0] = value_acc

    @pl.when(reach_ref[block] == 0)
    def _():
        dk_ref[...] = jnp.zeros(dk_ref.shape, jnp.float32)
        dv_ref[...] = jnp.zeros(dv_ref.shape, jnp.float32)

    @pl.when(block == last)
    def _():
        for h in range(heads):
            dq_ref[:, h * head:(h + 1) * head] = dq_scr[h]


def flash_backward(reach, own, queries, out_grad, key_stack, value_stack, lse, delta,
                   *, heads, head, scale, interpret=False):
    rows, width = queries.shape
    blocks = key_stack.shape[0]
    kv_width = key_stack.shape[2]
    groups = width // (heads * head)
    kernel = functools.partial(_bwd_kernel, heads=heads, head=head, scale=scale)
    grid_spec = pltpu.PrefetchScalarGridSpec(
        num_scalar_prefetch=2,
        grid=(groups, blocks),
        in_specs=[
            pl.BlockSpec((rows, heads * head), lambda g, b, r, o: (0, g)),
            pl.BlockSpec((rows, heads * head), lambda g, b, r, o: (0, g)),
            pl.BlockSpec((1, rows, head), lambda g, b, r, o: (b, 0, g)),
            pl.BlockSpec((1, rows, head), lambda g, b, r, o: (b, 0, g)),
            pl.BlockSpec((heads, rows, 1), lambda g, b, r, o: (g, 0, 0)),
            pl.BlockSpec((heads, rows, 1), lambda g, b, r, o: (g, 0, 0)),
        ],
        out_specs=[
            pl.BlockSpec((rows, heads * head), lambda g, b, r, o: (0, g)),
            pl.BlockSpec((1, rows, head), lambda g, b, r, o: (b, 0, g)),
            pl.BlockSpec((1, rows, head), lambda g, b, r, o: (b, 0, g)),
        ],
        scratch_shapes=[pltpu.VMEM((heads, rows, head), jnp.float32)],
    )
    return pl.pallas_call(
        kernel,
        grid_spec=grid_spec,
        out_shape=[
            jax.ShapeDtypeStruct((rows, width), jnp.float32),
            jax.ShapeDtypeStruct((blocks, rows, kv_width), jnp.float32),
            jax.ShapeDtypeStruct((blocks, rows, kv_width), jnp.float32),
        ],
        compiler_params=pltpu.CompilerParams(dimension_semantics=("arbitrary", "arbitrary")),
        interpret=interpret,
    )(reach, own, queries, out_grad, key_stack, value_stack, lse, delta)


def body(query_input, key_input, value_input, out_grad, query_bias, key_bias, value_bias, parents):
    tree_count, row_count, query_width = query_input.shape
    key_width = key_input.shape[2]
    score_scale = HEAD ** (-0.5)
    group_size = Q_HEADS // KV_HEADS
    devices = lax.axis_size("ctx")
    device_index = lax.axis_index("ctx")
    raw_pair = jnp.stack([key_input, value_input], axis=2)
    gathered = lax.all_gather(raw_pair, "ctx", axis=1, tiled=True)
    ancestors = jax.vmap(ancestry)(parents)
    block_depth = jnp.sum(ancestors, axis=2) - 1.0
    offsets = jnp.arange(row_count, dtype=jnp.float32)
    all_places = block_depth[:, :, None] * row_count + offsets[None, None, :]
    own_places = lax.dynamic_index_in_dim(all_places, device_index, 1, keepdims=False)
    own_reach = lax.dynamic_index_in_dim(ancestors, device_index, 1, keepdims=False)
    queries = rotate(
        (query_input.astype(jnp.float32) + query_bias).reshape(
            tree_count, row_count, Q_HEADS, HEAD
        ),
        own_places,
        1.0,
    ).astype(jnp.bfloat16)
    tree_length = row_count * devices
    flat_places = all_places.reshape(tree_count, tree_length)
    key_piece = rotate(
        (gathered[:, :, 0].astype(jnp.float32) + key_bias).reshape(
            tree_count, tree_length, KV_HEADS, HEAD
        ),
        flat_places,
        1.0,
    ).astype(jnp.bfloat16)
    value_piece = (
        (gathered[:, :, 1].astype(jnp.float32) + value_bias)
        .astype(jnp.bfloat16)
        .reshape(tree_count, tree_length, KV_HEADS, HEAD)
    )
    reach_flags = (own_reach[0] > 0.5).astype(jnp.int32)
    own_block = jnp.reshape(device_index, (1,)).astype(jnp.int32)
    flat_queries = queries.reshape(row_count, query_width)
    flat_grads = out_grad.reshape(row_count, query_width)
    key_stack = key_piece.reshape(devices, row_count, key_width)
    value_stack = value_piece.reshape(devices, row_count, key_width)
    out_rows, log_total = flash_forward(
        reach_flags, own_block, flat_queries, key_stack, value_stack,
        heads=group_size, head=HEAD, scale=score_scale,
    )
    row_delta = jnp.sum(
        (flat_grads.astype(jnp.float32) * out_rows.astype(jnp.float32)).reshape(
            row_count, Q_HEADS, HEAD
        ),
        axis=-1,
    )
    row_delta = jnp.transpose(row_delta, (1, 0))[:, :, None]
    query_sum, key_parts, value_parts = flash_backward(
        reach_flags, own_block, flat_queries, flat_grads, key_stack, value_stack,
        log_total, row_delta, heads=group_size, head=HEAD, scale=score_scale,
    )
    key_parts = rotate(
        key_parts.reshape(devices, row_count, KV_HEADS, HEAD), all_places[0], -1.0
    ).reshape(devices, row_count, key_width)
    key_total = jnp.sum(key_parts, axis=(0, 1))
    value_total = jnp.sum(value_parts, axis=(0, 1))
    stacked = jnp.stack([key_parts, value_parts], axis=2).astype(jnp.bfloat16)
    stacked = stacked.reshape(devices, tree_count, row_count, 2, key_width)
    arrived = lax.all_to_all(stacked, "ctx", 0, 0, tiled=True)
    own_grads = jnp.sum(arrived.astype(jnp.float32), axis=0)
    key_full = own_grads[:, :, 0]
    value_full = own_grads[:, :, 1]
    query_full = rotate(
        query_sum.reshape(tree_count, row_count, Q_HEADS, HEAD), own_places, -1.0
    ).reshape(tree_count, row_count, query_width)
    attended = out_rows.reshape(tree_count, row_count, query_width)
    query_total = jnp.sum(query_full, axis=(0, 1))
    query_total, key_total, value_total = lax.psum(
        (query_total, key_total, value_total), ("dp", "ctx")
    )
    return (attended, query_full, key_full, value_full, query_total, key_total, value_total)


def solution(mesh):
    placed = (
        P("dp", "ctx", None),
        P("dp", "ctx", None),
        P("dp", "ctx", None),
        P("dp", "ctx", None),
        P(),
        P(),
        P(),
        P("dp", None),
    )
    return jax.shard_map(
        body,
        mesh=mesh,
        in_specs=placed,
        out_specs=(
            P("dp", "ctx", None),
            P("dp", "ctx", None),
            P("dp", "ctx", None),
            P("dp", "ctx", None),
            P(),
            P(),
            P(),
        ),
        check_vma=False,
    )
```

time: 674 us -> 826 us (1.23)
  starting transfers between devices: 0.08 us -> 251 us
  Pallas kernels: 0 us -> 160 us
  blocking collectives: 325 us -> 193 us
  local copies, waits for them, and re-layouts: 131 us -> 63.2 us
  loops' own time: 57 us -> 0 us
  matrix products: 14.5 us -> 0.66 us
  other arithmetic: 84.4 us -> 95 us
    all_to_all x0 -> x1, starting transfers between devices: none -> 251 us  [body(): arrived = lax.all_to_all(stacked, 'ctx', 0, 0, tiled=True)]
    pallas_call x0 -> x2, Pallas kernels: none -> 160 us  [the longest x1 83.8 us: flash_backward(): pl.pallas_call(kernel, grid_spec=grid_spec, out_shape=[jax.ShapeDtypeStru...]
    psum x1, blocking collectives: 325 us -> 193 us  [body(): lax.psum((query_total, key_total, value_total), ('dp', 'ctx'))]
    another operation x34 -> x0, loops' own time: 57 us -> none  [the longest x1 42.2 us: body(): lax.scan(one_grad_block, jnp.zeros((tree_count, row_count, KV_HEADS, grou...]
    dynamic_update_slice x32 -> x0, local copies, waits for them, and re-layouts: 27.1 us -> none  [body(): lax.scan(one_grad_block, jnp.zeros((tree_count, row_count, KV_HEADS, grou...]
    gt x32 -> x0, other arithmetic: 20 us -> none  [the longest x16 10.3 us: one_grad_block(): reach_values > 0.5]
    another operation x7 -> x2, local copies, waits for them, and re-layouts: 30.5 us -> 15.7 us  [body(): stacked = jnp.stack([key_parts, value_parts], axis=2).astype(jnp.bfloat16)]
    dot_general x7 -> x0, matrix products: 13.8 us -> none  [the longest x1 2.72 us: tile_forward(): jnp.einsum('tqghk,tkgd->tqghd', weights.astype(jnp.bfloat16), value_tile,...]
  transfers between devices with their start and end apart: 2 -> 2, of which waited for: 1 -> 1; matrix products, arithmetic and copies ran while one was open for 9% -> 6% of each run, Pallas kernels for 0% -> 0%
where the time goes in v2:
time: 826 us; the launch traced here: 825 us
  starting transfers between devices  251 us (30%)
  blocking collectives  193 us (23%)
  Pallas kernels  160 us (19%)
  other arithmetic  95 us (12%)
  local copies, waits for them, and re-layouts  63.2 us (8%)
  waiting for transfers between devices  49 us (6%)
  between operations  14.6 us (2%)
    all_to_all x1, starting transfers between devices, body(): arrived = lax.all_to_all(stacked, 'ctx', 0, 0, tiled=True)  251 us
    psum x1, blocking collectives, body(): lax.psum((query_total, key_total, value_total), ('dp', 'ctx'))  193 us
    pallas_call x1, Pallas kernels, flash_backward(): pl.pallas_call(kernel, grid_spec=grid_spec, out_shape=[jax.ShapeDtypeStru...  83.8 us
    pallas_call x1, Pallas kernels, flash_forward(): pl.pallas_call(kernel, grid_spec=grid_spec, out_shape=[jax.ShapeDtypeStru...  75.7 us
    all_gather x1, waiting for transfers between devices, body(): gathered = lax.all_gather(raw_pair, 'ctx', axis=1, tiled=True)  49 us
    unnamed x20, local copies, waits for them, and re-layouts  29 us
  transfers between devices with their start and end apart: 2, of which 1 were waited for; matrix products, arithmetic and copies ran while one was open for 6% of the time, Pallas kernels for 0%

profile of v2, /device:TPU:1, one launch (start us, length us, event | category | flops | bytes accessed | tf_op | source)
XLA Modules:
  0.0 825.3 jit_solution(3048462310304876957)
XLA Ops:
  11.2 2.8 copy.21
  16.3 5.0 subtract_convert_fusion.1
  22.5 3.1 copy.28
  26.3 5.5 multiply_cosine_fusion
  31.8 3.7 multiply_cosine_fusion.1
  35.5 49.0 %all-gather.2.cloned.1.call-done = bf16[1,2048,2,1024]{3,1,2,0:T(8,128)(2,1)} async-done(((bf16[1,128,2,1024]{3,1,2,0:T(8,128)(2,1)}), bf16[1,2048,2,1024]{3,1,2,0:T(8,128)(2,1)}) %all-gather.2.cloned.1.call-update) | async-done | bytes 8388624 | tf_op jit(solution)/shard_map/all_gather | solution.py:229
  84.5 5.5 fusion.9
  90.0 5.3 copy.23
  95.3 3.8 bitcast_add_fusion
  99.1 4.5 subtract_convert_fusion
  103.6 5.2 pad_maximum_fusion.2
  108.8 7.3 convert_element_type.124.k_ref
  116.1 5.5 fusion.v_ref
  121.6 75.7 %shard_map.138 = (bf16[128,8192]{1,0:T(8,128)(2,1)}, f32[64,128,1]{2,1,0:T(8,128)}) custom-call(s32[16]{0:T(128)} %fusion.5.reach_ref, s32[1]{0:T(128)} %bitcast.3.own_ref, bf16[128,8192]{1,0:T(8,128)(2,1)} %bitcast.77, bf16[16,128,1024]{2,1,0:T(8,128)(2,1)} %convert_element_type.124.k_ref, bf16[16,128,1024]{2,1,0:T(8,128)(2,1)} %fusion.v_ref), custom_call_target="tpu_custom_call" | custom-call | tf_op jit(solution)/shard_map/pallas_call | solution.py:124
  202.1 3.3 reduce_sum.61
  205.4 4.6 copy.17.delta_ref
  210.0 83.8 %shard_map.139 = (f32[128,8192]{1,0:T(8,128)}, f32[16,128,1024]{2,1,0:T(8,128)}, f32[16,128,1024]{2,1,0:T(8,128)}) custom-call(s32[16]{0:T(128)} %fusion.5.reach_ref, s32[1]{0:T(128)} %bitcast.3.own_ref, bf16[128,8192]{1,0:T(8,128)(2,1)} %bitcast.78, bf16[128,8192]{1,0:T(8,128)(2,1)} %bitcast.83, bf16[16,128,1024]{2,1,0:T(8,128)(2,1)} %convert_element_type.124.k_ref, ...), custom_call_target="tpu_custom_call" | custom-call | tf_op jit(solution)/shard_map/pallas_call | solution.py:208
  293.8 8.9 %copy.26 = f32[256,8,8,128]{3,2,1,0:T(8,128)} copy(f32[256,8,8,128]{3,1,2,0:T(8,128)} %bitcast.82) | data formatting | bytes 16777216
  302.8 3.1 fusion.8
  305.9 10.2 %multiply_subtract_fusion = (f32[16,128,8,64]{3,2,1,0:T(8,128)S(1)}, f32[16,128,8,64]{3,2,1,0:T(8,128)}) fusion(f32[16,128,8,128]{3,2,1,0:T(8,128)} %bitcast.73, f32[16,128,64]{2,1,0:T(8,128)S(1)} %copy-done.3, f32[16,128,64]{2,1,0:T(8,128)S(1)} %get-tuple-element.36), kind=kLoop, calls=%fused_computation.8 | loop fusion | flops 6291456 | bytes 17825792 | tf_op jit(solution)/shard_map/sub | solution.py:45
  316.1 3.2 copy-done
  319.3 5.7 fusion.2
  325.0 7.5 stack.20
  332.5 7.5 pad_maximum_fusion.1
  340.0 8.2 copy.18
  348.2 250.6 %all-to-all-start = ((bf16[16,1,128,2,1024]{4,2,3,1,0:T(8,128)(2,1)}), bf16[16,1,128,2,1024]{4,2,3,1,0:T(8,128)(2,1)}, u32[]{:S(2)}, u32[]{:S(2)}) async-start(bf16[16,1,128,2,1024]{4,2,3,1,0:T(8,128)(2,1)} %copy.18), calls=%async_computation | async-start | bytes 16777216 | tf_op jit(solution)/shard_map/all_to_all | solution.py:285
  598.8 2.9 copy.25
  603.7 3.2 fusion.7
  606.9 4.9 reshape.592
  611.8 7.0 fusion.1
  618.8 192.6 %all-reduce = (f32[8192]{0:T(1024)}, f32[1024]{0:T(1024)}, f32[1024]{0:T(1024)}) all-reduce(f32[8192]{0:T(1024)S(1)} %bitcast.90, f32[1024]{0:T(1024)S(1)} %bitcast.93, f32[1024]{0:T(1024)S(1)} %get-tuple-element.26), channel_id=1, replica_groups=mesh['dp'=8,'ctx'=16] {'dp','ctx'}, use_global_device_ids=true, to_apply=%region_4.5 | all-reduce | flops 10240 | bytes 81920 | tf_op jit(solution)/shard_map/psum | solution.py:294
  811.4 5.5 convert_reduce_fusion
  (38 shorter events, 15.9 us)
Async XLA Ops:
  7.2 77.3 %all-gather.2.cloned.1.call-start = ((), (), s32[]{:S(2)}) async-start(), calls=%async_computation.1 | async-start | bytes 8912896 | tf_op jit(solution)/shard_map/all_gather | solution.py:229
  11.2 2.8 copy-start.6
  90.0 5.3 copy-start.4
  108.8 7.3 copy-start.5
  121.6 75.7 %copy-start.2 = (bf16[1,128,8192]{2,1,0:T(8,128)(2,1)S(1)}, bf16[1,128,8192]{2,1,0:T(8,128)(2,1)}, u32[]{:S(2)}) copy-start(bf16[1,128,8192]{2,1,0:T(8,128)(2,1)} %param.11) | copy-start | bytes 6291460
  293.8 8.9 %copy-start.1 = (f32[16,128,1024]{2,1,0:T(8,128)S(1)}, f32[16,128,1024]{2,1,0:T(8,128)}, u32[]{:S(2)}) copy-start(f32[16,128,1024]{2,1,0:T(8,128)} %get-tuple-element.16) | copy-start | bytes 25165828
  302.8 3.1 copy-start.3
  316.1 3.2 copy-start
  348.2 463.2 %all-to-all-start = ((bf16[16,1,128,2,1024]{4,2,3,1,0:T(8,128)(2,1)}), bf16[16,1,128,2,1024]{4,2,3,1,0:T(8,128)(2,1)}, u32[]{:S(2)}, u32[]{:S(2)}) async-start(bf16[16,1,128,2,1024]{4,2,3,1,0:T(8,128)(2,1)} %copy.18), calls=%async_computation | async-start | bytes 16777216 | tf_op jit(solution)/shard_map/all_to_all | solution.py:285
Sparse Core Ops, SparseCore 0:
  10.7 73.7 all-gather.1
